TPU v7x, 256 devices: a whole 4x4x8 slice. The times are simulated.
256 devices in a mesh: pair: 32 (over y, x, core), lam: 8 (over z).
Axes of the slice: x: 4, y: 4, z: 8, core: 2. Of those that a mesh axis runs over, the one named last changes fastest.
Arguments:
- integrals: bfloat16 [32, 64, 4, 64, 1024], P('pair', 'lam'), may hold values from -0.119628906 to 0.119628906
- tile_pair: int32 [32, 64], P('pair', 'lam'), may hold values from 0 to 15, as said below
- tile_lam: int32 [32, 64], P('pair', 'lam'), may hold values from 0 to 15, as said below
- tile_count: int32 [32, 8], P('pair', 'lam'), may hold values from 1 to 8, as said below
- mu_index: int32 [2048], P('pair'), may hold values from 0 to 1023
- nu_index: int32 [2048], P('pair'), may hold values from 0 to 1023
- occupied_coef: bfloat16 [1024, 16], replicated, may hold values from -1.5 to 1.5
- virtual_coef: bfloat16 [1024, 1280], replicated, may hold values from -1.5 to 1.5
Outputs:
- orbital_integrals: float32 [16, 1280, 20480], P('lam', 'pair')
Inputs may be any that keep to these rules, and one draw needn't show every extreme that they name: On every device the live and dead slots name distinct pairs of (tile_pair, tile_lam); tile_pair lies in 0 to 15. On lam index l every slot's tile_lam lies in l * 2 to (l + 1) * 2 - 1. Slots from tile_count on are dead and their integrals are ignored; some device has all 8 slots live.
All inputs are finite; a program needn't handle non-finite values.
Results may differ from a plain program's by a relative error of at most 0.0049.
Values may be sent and summed in bfloat16 or wider, within the bound.
No kernel may reach another device: no remote copies, remote signals or barrier semaphores. Data moves between devices by JAX's collectives and lax.ppermute only.
A program may use at most 128 MiB of HBM per device.

v0:
```python
import math
import jax
import jax.numpy as jnp
from jax import lax
from jax.sharding import PartitionSpec as P


def tile_pass(partial_value, tile_group, occ_columns):
    tile_data, pair_list, lam_list, live_total = tile_group
    tile_rows = tile_data.shape[1]
    tile_depth = tile_data.shape[2]

    def add_tile(slot_index, running):
        row_start = pair_list[slot_index] * tile_rows
        occ_rows = lax.dynamic_slice_in_dim(
            occ_columns, lam_list[slot_index] * tile_depth, tile_depth, 0
        )
        contrib = jnp.einsum(
            "rls,lj->jrs", tile_data[slot_index], occ_rows, preferred_element_type=jnp.float32
        )
        current = lax.dynamic_slice_in_dim(running, row_start, tile_rows, 1)
        return lax.dynamic_update_slice_in_dim(running, current + contrib, row_start, 1)

    return lax.fori_loop(0, live_total, add_tile, partial_value)


def on_device(
    integrals, tile_pair, tile_lam, tile_count, mu_index, nu_index, occupied_coef, virtual_coef
):
    lam_count = lax.axis_size("lam")
    pair_count = lax.axis_size("pair")
    occ_total = occupied_coef.shape[1]
    vir_total = virtual_coef.shape[1]
    basis_count = occupied_coef.shape[0]
    rows_here = mu_index.shape[0]
    tile_data = integrals[0]
    pair_list = tile_pair[0]
    lam_list = tile_lam[0]
    live_total = tile_count[0, 0]
    tile_groups = (tile_data, pair_list, lam_list, live_total)
    occ_share = occ_total // lam_count
    partial_value = jnp.zeros((occupied_coef.shape[1], rows_here, basis_count), jnp.float32)
    partial_value = tile_pass(partial_value, tile_groups, occupied_coef)
    summed = lax.psum(partial_value, "lam")
    own_half = lax.dynamic_slice_in_dim(summed, lax.axis_index("lam") * occ_share, occ_share, 0)
    vir_share = vir_total // pair_count
    half_low = own_half.astype(jnp.bfloat16).reshape(occ_share * rows_here, basis_count)
    mixed = jnp.dot(half_low, virtual_coef, preferred_element_type=jnp.float32)
    mixed = mixed.astype(jnp.bfloat16).reshape(occ_share, rows_here, pair_count, vir_share)
    first_all, second_all = (
        lax.all_gather(mu_index, "pair", axis=0, tiled=True),
        lax.all_gather(nu_index, "pair", axis=0, tiled=True),
    )
    received = lax.all_to_all(mixed, "pair", split_axis=2, concat_axis=1, tiled=True)
    item_count = received.shape[0]
    total_rows = received.shape[1]
    column_count = received.shape[3]
    mixed_rows = received.reshape(item_count, total_rows, column_count)
    row_block = math.gcd(total_rows, 256)

    def add_rows(running, row_start):
        occ_rows = jnp.take(
            occupied_coef, lax.dynamic_slice_in_dim(first_all, row_start, row_block), axis=0
        ).astype(jnp.float32)
        vir_rows = jnp.take(
            virtual_coef, lax.dynamic_slice_in_dim(second_all, row_start, row_block), axis=0
        ).astype(jnp.float32)
        weights = (
            (occ_rows[:, :, None] * vir_rows[:, None, :])
            .astype(jnp.bfloat16)
            .reshape(row_block, occ_total * vir_total)
        )
        mixed_piece = lax.dynamic_slice_in_dim(mixed_rows, row_start, row_block, 1)
        return (
            running
            + jnp.einsum("qrb,rk->qbk", mixed_piece, weights, preferred_element_type=jnp.float32),
            None,
        )

    start_total = jnp.zeros((item_count, column_count, occ_total * vir_total), jnp.float32)
    result, _ = lax.scan(
        add_rows, start_total, jnp.arange(0, total_rows, row_block, dtype=jnp.int32)
    )
    return result


def solution(mesh):
    placed = (
        P("pair", "lam", None, None, None),
        P("pair", "lam"),
        P("pair", "lam"),
        P("pair", "lam"),
        P("pair"),
        P("pair"),
        P(),
        P(),
    )
    return jax.shard_map(
        on_device, mesh=mesh, in_specs=placed, out_specs=P("lam", "pair", None), check_vma=False
    )
```

profile of v0, /device:TPU:32, one launch (start us, length us, event | category | flops | bytes accessed | tf_op | source)
XLA Modules:
  0.0 604.5 jit_solution(9514965633434375320)
XLA Ops:
  0.0 2.5 broadcast_in_dim.33.clone
  2.5 27.5 %while.21 = (s32[]{:T(128)}, f32[16,64,1024]{2,1,0:T(8,128)}, s32[]{:T(128)}, s32[8]{0:T(128)S(1)}, s32[8]{0:T(128)S(1)}, /*index=5*/bf16[1024,16]{0,1:T(8,128)(...) while((s32[]{:T(128)}, f32[16,64,1024]{2,1,0:T(8,128)}, ...), condition=%wide.region_1.0_spmd, body=%wide.region_0.0_spmd.sunk | while | flops 8454157 | bytes 2101547 | solution.py:24
  7.0 1.4 convolution_add_fusion.4
  13.7 1.4 convolution_add_fusion.4
  20.5 1.4 convolution_add_fusion.4
  27.2 1.4 convolution_add_fusion.4
  30.1 110.6 %all-reduce.4 = bf16[16,64,1024]{2,1,0:T(8,128)(2,1)} all-reduce(f32[16,64,1024]{2,1,0:T(8,128)} %get-tuple-element.85), channel_id=1, replica_groups=mesh['pair'=32,'lam'=8] {'lam'}, use_global_device_ids=true, to_apply=%region_2.0 | all-reduce | flops 1048576 | bytes 6291456 | tf_op jit(solution)/shard_map/psum | solution.py:44
  143.2 1.3 reshape.62
  145.6 13.8 %all-to-all-start = ((bf16[32,2,2560]{2,1,0:T(2,128)(2,1)}), bf16[32,2,2560]{2,1,0:T(2,128)(2,1)}, u32[]{:S(2)}, u32[]{:S(2)}) async-start(bf16[32,2,2560]{2,1,0:T(2,128)(2,1)} %reshape.99), calls=%async_computation | async-start | bytes 655360 | tf_op jit(solution)/shard_map/all_to_all | solution.py:54
  162.0 128.6 %all-reduce.2 = (s32[2048]{0:T(1024)}, s32[2048]{0:T(1024)}) all-reduce(s32[2048]{0:T(1024)S(1)} %dynamic-update-slice, s32[2048]{0:T(1024)S(1)} %dynamic-update-slice.1), channel_id=1, replica_groups=mesh['pair'=32,'lam'=8] {'pair'}, use_global_device_ids=true, to_apply=%add | all-reduce | flops 4096 | bytes 32768
  290.6 1.4 reshape.100
  292.6 1.2 reshape.63
  293.9 310.6 %while.22 = (s32[]{:T(128)}, f32[2,40,20480]{2,1,0:T(8,128)}, s32[8]{0:T(128)S(1)}, bf16[2,2048,40]{1,2,0:T(8,128)(2,1)}, s32[2048]{0:T(1024)}, /*index=5*/bf16[...) while((s32[]{:T(128)}, f32[2,40,20480]{2,1,0:T(8,128)}, ...), condition=%wide.region_4.5_spmd.clone, body=%wide.region_3.4_spmd.clone.sunk | while | flops 853292032 | bytes 59753956 | solution.py:81
  297.4 1.3 gather_fusion
  298.7 1.2 select_convert_fusion.4
  300.9 6.7 %multiply_convert_fusion.2 = bf16[256,16,1280]{2,1,0:T(8,128)(2,1)} fusion(f32[256,1280]{1,0:T(8,128)} %select_convert_fusion.4, f32[256,16]{1,0:T(8,128)S(1)} %select_convert_fusion.5), kind=kLoop, calls=%fused_computation.11.clone.1 | loop fusion | flops 10485760 | bytes 11812864 | tf_op jit(solution)/shard_map/while/body/eval_jaxpr/convert_element_type | solution.py:70
  307.6 14.8 %reshape.110 = bf16[256,20480,1]{1,0,2:T(8,128)(2,1)} reshape(bf16[256,16,1280]{2,1,0:T(8,128)(2,1)} %multiply_convert_fusion.2) | data formatting | bytes 20971520 | tf_op jit(solution)/shard_map/while/body/eval_jaxpr/convert_element_type | solution.py:70
  322.3 8.8 %convolution_add_fusion.5 = f32[2,40,20480]{2,1,0:T(8,128)} fusion(bf16[256,20480,1]{1,0,2:T(8,128)(2,1)} %reshape.110, f32[2,40,20480]{2,1,0:T(8,128)} %get-tuple-element.331, pred[]{:T(512)S(6)} %compare.3, bf16[2,2048,40]{1,2,0:T(8,128)(2,1)} %get-tuple-element.344, s32[]{:T(128)S(6)} %select_n.68), kind=kOutput, calls=%fused_computation.10.clone.1 | convolution fusion | flops 842137600 | bytes 23633924 | tf_op jit(solution)/shard_map/while/body/eval_jaxpr/qrb,rk->qbk/dot_general | solution.py:76
  334.6 1.3 gather_fusion
  335.9 1.2 select_convert_fusion.4
  338.1 6.7 %multiply_convert_fusion.2 = bf16[256,16,1280]{2,1,0:T(8,128)(2,1)} fusion(f32[256,1280]{1,0:T(8,128)} %select_convert_fusion.4, f32[256,16]{1,0:T(8,128)S(1)} %select_convert_fusion.5), kind=kLoop, calls=%fused_computation.11.clone.1 | loop fusion | flops 10485760 | bytes 11812864 | tf_op jit(solution)/shard_map/while/body/eval_jaxpr/convert_element_type | solution.py:70
  344.8 14.8 %reshape.110 = bf16[256,20480,1]{1,0,2:T(8,128)(2,1)} reshape(bf16[256,16,1280]{2,1,0:T(8,128)(2,1)} %multiply_convert_fusion.2) | data formatting | bytes 20971520 | tf_op jit(solution)/shard_map/while/body/eval_jaxpr/convert_element_type | solution.py:70
  359.5 10.6 %convolution_add_fusion.5 = f32[2,40,20480]{2,1,0:T(8,128)} fusion(bf16[256,20480,1]{1,0,2:T(8,128)(2,1)} %reshape.110, f32[2,40,20480]{2,1,0:T(8,128)} %get-tuple-element.331, pred[]{:T(512)S(6)} %compare.3, bf16[2,2048,40]{1,2,0:T(8,128)(2,1)} %get-tuple-element.344, s32[]{:T(128)S(6)} %select_n.68), kind=kOutput, calls=%fused_computation.10.clone.1 | convolution fusion | flops 842137600 | bytes 23633924 | tf_op jit(solution)/shard_map/while/body/eval_jaxpr/qrb,rk->qbk/dot_general | solution.py:76
  373.7 1.2 gather_fusion
  377.1 6.7 %multiply_convert_fusion.2 = bf16[256,16,1280]{2,1,0:T(8,128)(2,1)} fusion(f32[256,1280]{1,0:T(8,128)} %select_convert_fusion.4, f32[256,16]{1,0:T(8,128)S(1)} %select_convert_fusion.5), kind=kLoop, calls=%fused_computation.11.clone.1 | loop fusion | flops 10485760 | bytes 11812864 | tf_op jit(solution)/shard_map/while/body/eval_jaxpr/convert_element_type | solution.py:70
  383.8 14.8 %reshape.110 = bf16[256,20480,1]{1,0,2:T(8,128)(2,1)} reshape(bf16[256,16,1280]{2,1,0:T(8,128)(2,1)} %multiply_convert_fusion.2) | data formatting | bytes 20971520 | tf_op jit(solution)/shard_map/while/body/eval_jaxpr/convert_element_type | solution.py:70
  398.6 10.6 %convolution_add_fusion.5 = f32[2,40,20480]{2,1,0:T(8,128)} fusion(bf16[256,20480,1]{1,0,2:T(8,128)(2,1)} %reshape.110, f32[2,40,20480]{2,1,0:T(8,128)} %get-tuple-element.331, pred[]{:T(512)S(6)} %compare.3, bf16[2,2048,40]{1,2,0:T(8,128)(2,1)} %get-tuple-element.344, s32[]{:T(128)S(6)} %select_n.68), kind=kOutput, calls=%fused_computation.10.clone.1 | convolution fusion | flops 842137600 | bytes 23633924 | tf_op jit(solution)/shard_map/while/body/eval_jaxpr/qrb,rk->qbk/dot_general | solution.py:76
  412.8 1.3 gather_fusion
  414.0 1.2 select_convert_fusion.4
  416.2 6.7 %multiply_convert_fusion.2 = bf16[256,16,1280]{2,1,0:T(8,128)(2,1)} fusion(f32[256,1280]{1,0:T(8,128)} %select_convert_fusion.4, f32[256,16]{1,0:T(8,128)S(1)} %select_convert_fusion.5), kind=kLoop, calls=%fused_computation.11.clone.1 | loop fusion | flops 10485760 | bytes 11812864 | tf_op jit(solution)/shard_map/while/body/eval_jaxpr/convert_element_type | solution.py:70
  422.9 14.8 %reshape.110 = bf16[256,20480,1]{1,0,2:T(8,128)(2,1)} reshape(bf16[256,16,1280]{2,1,0:T(8,128)(2,1)} %multiply_convert_fusion.2) | data formatting | bytes 20971520 | tf_op jit(solution)/shard_map/while/body/eval_jaxpr/convert_element_type | solution.py:70
  437.7 10.6 %convolution_add_fusion.5 = f32[2,40,20480]{2,1,0:T(8,128)} fusion(bf16[256,20480,1]{1,0,2:T(8,128)(2,1)} %reshape.110, f32[2,40,20480]{2,1,0:T(8,128)} %get-tuple-element.331, pred[]{:T(512)S(6)} %compare.3, bf16[2,2048,40]{1,2,0:T(8,128)(2,1)} %get-tuple-element.344, s32[]{:T(128)S(6)} %select_n.68), kind=kOutput, calls=%fused_computation.10.clone.1 | convolution fusion | flops 842137600 | bytes 23633924 | tf_op jit(solution)/shard_map/while/body/eval_jaxpr/qrb,rk->qbk/dot_general | solution.py:76
  451.8 1.3 gather_fusion
  455.3 6.7 %multiply_convert_fusion.2 = bf16[256,16,1280]{2,1,0:T(8,128)(2,1)} fusion(f32[256,1280]{1,0:T(8,128)} %select_convert_fusion.4, f32[256,16]{1,0:T(8,128)S(1)} %select_convert_fusion.5), kind=kLoop, calls=%fused_computation.11.clone.1 | loop fusion | flops 10485760 | bytes 11812864 | tf_op jit(solution)/shard_map/while/body/eval_jaxpr/convert_element_type | solution.py:70
  462.0 14.8 %reshape.110 = bf16[256,20480,1]{1,0,2:T(8,128)(2,1)} reshape(bf16[256,16,1280]{2,1,0:T(8,128)(2,1)} %multiply_convert_fusion.2) | data formatting | bytes 20971520 | tf_op jit(solution)/shard_map/while/body/eval_jaxpr/convert_element_type | solution.py:70
  476.7 10.6 %convolution_add_fusion.5 = f32[2,40,20480]{2,1,0:T(8,128)} fusion(bf16[256,20480,1]{1,0,2:T(8,128)(2,1)} %reshape.110, f32[2,40,20480]{2,1,0:T(8,128)} %get-tuple-element.331, pred[]{:T(512)S(6)} %compare.3, bf16[2,2048,40]{1,2,0:T(8,128)(2,1)} %get-tuple-element.344, s32[]{:T(128)S(6)} %select_n.68), kind=kOutput, calls=%fused_computation.10.clone.1 | convolution fusion | flops 842137600 | bytes 23633924 | tf_op jit(solution)/shard_map/while/body/eval_jaxpr/qrb,rk->qbk/dot_general | solution.py:76
  490.9 1.2 gather_fusion
  494.3 6.7 %multiply_convert_fusion.2 = bf16[256,16,1280]{2,1,0:T(8,128)(2,1)} fusion(f32[256,1280]{1,0:T(8,128)} %select_convert_fusion.4, f32[256,16]{1,0:T(8,128)S(1)} %select_convert_fusion.5), kind=kLoop, calls=%fused_computation.11.clone.1 | loop fusion | flops 10485760 | bytes 11812864 | tf_op jit(solution)/shard_map/while/body/eval_jaxpr/convert_element_type | solution.py:70
  501.0 14.8 %reshape.110 = bf16[256,20480,1]{1,0,2:T(8,128)(2,1)} reshape(bf16[256,16,1280]{2,1,0:T(8,128)(2,1)} %multiply_convert_fusion.2) | data formatting | bytes 20971520 | tf_op jit(solution)/shard_map/while/body/eval_jaxpr/convert_element_type | solution.py:70
  515.8 10.6 %convolution_add_fusion.5 = f32[2,40,20480]{2,1,0:T(8,128)} fusion(bf16[256,20480,1]{1,0,2:T(8,128)(2,1)} %reshape.110, f32[2,40,20480]{2,1,0:T(8,128)} %get-tuple-element.331, pred[]{:T(512)S(6)} %compare.3, bf16[2,2048,40]{1,2,0:T(8,128)(2,1)} %get-tuple-element.344, s32[]{:T(128)S(6)} %select_n.68), kind=kOutput, calls=%fused_computation.10.clone.1 | convolution fusion | flops 842137600 | bytes 23633924 | tf_op jit(solution)/shard_map/while/body/eval_jaxpr/qrb,rk->qbk/dot_general | solution.py:76
  529.9 1.2 gather_fusion
  533.3 6.7 %multiply_convert_fusion.2 = bf16[256,16,1280]{2,1,0:T(8,128)(2,1)} fusion(f32[256,1280]{1,0:T(8,128)} %select_convert_fusion.4, f32[256,16]{1,0:T(8,128)S(1)} %select_convert_fusion.5), kind=kLoop, calls=%fused_computation.11.clone.1 | loop fusion | flops 10485760 | bytes 11812864 | tf_op jit(solution)/shard_map/while/body/eval_jaxpr/convert_element_type | solution.py:70
  540.0 14.8 %reshape.110 = bf16[256,20480,1]{1,0,2:T(8,128)(2,1)} reshape(bf16[256,16,1280]{2,1,0:T(8,128)(2,1)} %multiply_convert_fusion.2) | data formatting | bytes 20971520 | tf_op jit(solution)/shard_map/while/body/eval_jaxpr/convert_element_type | solution.py:70
  554.8 10.6 %convolution_add_fusion.5 = f32[2,40,20480]{2,1,0:T(8,128)} fusion(bf16[256,20480,1]{1,0,2:T(8,128)(2,1)} %reshape.110, f32[2,40,20480]{2,1,0:T(8,128)} %get-tuple-element.331, pred[]{:T(512)S(6)} %compare.3, bf16[2,2048,40]{1,2,0:T(8,128)(2,1)} %get-tuple-element.344, s32[]{:T(128)S(6)} %select_n.68), kind=kOutput, calls=%fused_computation.10.clone.1 | convolution fusion | flops 842137600 | bytes 23633924 | tf_op jit(solution)/shard_map/while/body/eval_jaxpr/qrb,rk->qbk/dot_general | solution.py:76
  568.9 1.2 gather_fusion
  572.4 6.7 %multiply_convert_fusion.2 = bf16[256,16,1280]{2,1,0:T(8,128)(2,1)} fusion(f32[256,1280]{1,0:T(8,128)} %select_convert_fusion.4, f32[256,16]{1,0:T(8,128)S(1)} %select_convert_fusion.5), kind=kLoop, calls=%fused_computation.11.clone.1 | loop fusion | flops 10485760 | bytes 11812864 | tf_op jit(solution)/shard_map/while/body/eval_jaxpr/convert_element_type | solution.py:70
  579.1 14.8 %reshape.110 = bf16[256,20480,1]{1,0,2:T(8,128)(2,1)} reshape(bf16[256,16,1280]{2,1,0:T(8,128)(2,1)} %multiply_convert_fusion.2) | data formatting | bytes 20971520 | tf_op jit(solution)/shard_map/while/body/eval_jaxpr/convert_element_type | solution.py:70
  593.8 10.6 %convolution_add_fusion.5 = f32[2,40,20480]{2,1,0:T(8,128)} fusion(bf16[256,20480,1]{1,0,2:T(8,128)(2,1)} %reshape.110, f32[2,40,20480]{2,1,0:T(8,128)} %get-tuple-element.331, pred[]{:T(512)S(6)} %compare.3, bf16[2,2048,40]{1,2,0:T(8,128)(2,1)} %get-tuple-element.344, s32[]{:T(128)S(6)} %select_n.68), kind=kOutput, calls=%fused_computation.10.clone.1 | convolution fusion | flops 842137600 | bytes 23633924 | tf_op jit(solution)/shard_map/while/body/eval_jaxpr/qrb,rk->qbk/dot_general | solution.py:76
  (128 shorter events, 44.8 us)
Async XLA Ops:
  0.0 2.5 copy-start.1
  0.0 2.5 copy-start.2
  30.1 111.7 %copy-start = (bf16[1024,1280]{1,0:T(8,128)(2,1)S(1)}, bf16[1024,1280]{1,0:T(8,128)(2,1)}, u32[]{:S(2)}) copy-start(bf16[1024,1280]{1,0:T(8,128)(2,1)} %param.19) | copy-start | bytes 7864324
  140.7 19.6 %copy-start.5 = (u32[256]{0:T(256)S(1)}, u32[256]{0:T(256)}, u32[]{:S(2)}) copy-start(u32[256]{0:T(256)} %constant.71) | copy-start | bytes 3076
  140.7 20.7 %copy-start.3 = (s32[64]{0:T(128)S(1)}, s32[64]{0:T(128)}, u32[]{:S(2)}) copy-start(s32[64]{0:T(128)} %param.16) | copy-start | bytes 772
  140.7 21.0 %copy-start.4 = (s32[64]{0:T(128)S(1)}, s32[64]{0:T(128)}, u32[]{:S(2)}) copy-start(s32[64]{0:T(128)} %param.17) | copy-start | bytes 772
  145.6 145.0 %all-to-all-start = ((bf16[32,2,2560]{2,1,0:T(2,128)(2,1)}), bf16[32,2,2560]{2,1,0:T(2,128)(2,1)}, u32[]{:S(2)}, u32[]{:S(2)}) async-start(bf16[32,2,2560]{2,1,0:T(2,128)(2,1)} %reshape.99), calls=%async_computation | async-start | bytes 655360 | tf_op jit(solution)/shard_map/all_to_all | solution.py:54
  293.9 3.5 copy-start.6
  322.3 8.8 %copy-start.7 = (s32[8]{0:T(128)S(1)}, s32[8]{0:T(128)}, u32[]{:S(2)}) copy-start(s32[8]{0:T(128)} %copy-done.6) | copy-start | bytes 100 | tf_op jit(solution)/shard_map/while
  331.1 3.5 copy-start.6
  359.5 10.6 %copy-start.7 = (s32[8]{0:T(128)S(1)}, s32[8]{0:T(128)}, u32[]{:S(2)}) copy-start(s32[8]{0:T(128)} %copy-done.6) | copy-start | bytes 100 | tf_op jit(solution)/shard_map/while
  370.2 3.5 copy-start.6
  398.6 10.6 %copy-start.7 = (s32[8]{0:T(128)S(1)}, s32[8]{0:T(128)}, u32[]{:S(2)}) copy-start(s32[8]{0:T(128)} %copy-done.6) | copy-start | bytes 100 | tf_op jit(solution)/shard_map/while
  409.2 3.5 copy-start.6
  437.7 10.6 %copy-start.7 = (s32[8]{0:T(128)S(1)}, s32[8]{0:T(128)}, u32[]{:S(2)}) copy-start(s32[8]{0:T(128)} %copy-done.6) | copy-start | bytes 100 | tf_op jit(solution)/shard_map/while
  448.3 3.5 copy-start.6
  476.7 10.6 %copy-start.7 = (s32[8]{0:T(128)S(1)}, s32[8]{0:T(128)}, u32[]{:S(2)}) copy-start(s32[8]{0:T(128)} %copy-done.6) | copy-start | bytes 100 | tf_op jit(solution)/shard_map/while
  487.4 3.5 copy-start.6
  515.8 10.6 %copy-start.7 = (s32[8]{0:T(128)S(1)}, s32[8]{0:T(128)}, u32[]{:S(2)}) copy-start(s32[8]{0:T(128)} %copy-done.6) | copy-start | bytes 100 | tf_op jit(solution)/shard_map/while
  526.4 3.5 copy-start.6
  554.8 10.6 %copy-start.7 = (s32[8]{0:T(128)S(1)}, s32[8]{0:T(128)}, u32[]{:S(2)}) copy-start(s32[8]{0:T(128)} %copy-done.6) | copy-start | bytes 100 | tf_op jit(solution)/shard_map/while
  565.4 3.5 copy-start.6
  593.8 10.6 %copy-start.7 = (s32[8]{0:T(128)S(1)}, s32[8]{0:T(128)}, u32[]{:S(2)}) copy-start(s32[8]{0:T(128)} %copy-done.6) | copy-start | bytes 100 | tf_op jit(solution)/shard_map/while
where the time goes:
time: 609 us; the launch traced here: 604 us
  blocking collectives  239 us (39%)
  local copies, waits for them, and re-layouts  166 us (27%)
  matrix products  89.1 us (15%)
  other arithmetic  70.6 us (12%)
  loops' own time  25.5 us (4%)
  starting transfers between devices  13.8 us (2%)
    unnamed x1, blocking collectives  129 us
    convert_element_type x8, local copies, waits for them, and re-layouts, add_rows(): weights = (occ_rows[:, :, None] * vir_rows[:, None, :]).astype(jnp.bfloat...  118 us
    psum x1, blocking collectives, on_device(): summed = lax.psum(partial_value, 'lam')  111 us
    dot_general x8, matrix products, add_rows(): jnp.einsum('qrb,rk->qbk', mixed_piece, weights, preferred_element_type=jn...  83.1 us
    convert_element_type x8, other arithmetic, add_rows(): weights = (occ_rows[:, :, None] * vir_rows[:, None, :]).astype(jnp.bfloat...  53.6 us
    another operation x1, loops' own time, on_device(): lax.scan(add_rows, start_total, jnp.arange(0, total_rows, row_block, dtyp...  16.6 us
    all_to_all x1, starting transfers between devices, on_device(): lax.all_to_all(mixed, 'pair', split_axis=2, concat_axis=1, tiled=True)  13.8 us
  transfers between devices with their start and end apart: 1, of which 0 were waited for; matrix products, arithmetic and copies ran while one was open for 0% of the time, Pallas kernels for 0%

commit v1 on v0

--- a/solution.py
+++ b/solution.py
@@ -41,7 +41,7 @@
     occ_share = occ_total // lam_count
     partial_value = jnp.zeros((occupied_coef.shape[1], rows_here, basis_count), jnp.float32)
     partial_value = tile_pass(partial_value, tile_groups, occupied_coef)
-    summed = lax.psum(partial_value, "lam")
+    summed = jnp.sum(lax.all_gather(partial_value, "lam"), axis=0)
     own_half = lax.dynamic_slice_in_dim(summed, lax.axis_index("lam") * occ_share, occ_share, 0)
     vir_share = vir_total // pair_count
     half_low = own_half.astype(jnp.bfloat16).reshape(occ_share * rows_here, basis_count)

time: 609 us -> 865 us (1.42)
  waiting for transfers between devices: 0.01 us -> 352 us
  blocking collectives: 239 us -> 129 us
  other arithmetic: 70.6 us -> 85 us
  between operations: 0.69 us -> 14.2 us
    all_gather x0 -> x1, waiting for transfers between devices: none -> 352 us  [on_device(): summed = jnp.sum(lax.all_gather(partial_value, 'lam'), axis=0)]
    psum x1 -> x0, blocking collectives: 111 us -> none  [on_device(): summed = lax.psum(partial_value, 'lam')]
    reduce_sum x0 -> x1, other arithmetic: none -> 14.3 us  [on_device(): summed = jnp.sum(lax.all_gather(partial_value, 'lam'), axis=0)]
  transfers between devices with their start and end apart: 1 -> 2, of which waited for: 0 -> 1; matrix products, arithmetic and copies ran while one was open for 0% -> 0% of each run, Pallas kernels for 0% -> 0%
where the time goes in v1:
time: 865 us; the launch traced here: 860 us
  waiting for transfers between devices  352 us (41%)
  local copies, waits for them, and re-layouts  158 us (18%)
  blocking collectives  129 us (15%)
  matrix products  92 us (11%)
  other arithmetic  85 us (10%)
  loops' own time  23.6 us (3%)
  between operations  14.2 us (2%)
    all_gather x1, waiting for transfers between devices, on_device(): summed = jnp.sum(lax.all_gather(partial_value, 'lam'), axis=0)  352 us
    unnamed x1, blocking collectives  129 us
    convert_element_type x8, local copies, waits for them, and re-layouts, add_rows(): weights = (occ_rows[:, :, None] * vir_rows[:, None, :]).astype(jnp.bfloat...  118 us
    dot_general x8, matrix products, add_rows(): jnp.einsum('qrb,rk->qbk', mixed_piece, weights, preferred_element_type=jn...  83.1 us
    convert_element_type x8, other arithmetic, add_rows(): weights = (occ_rows[:, :, None] * vir_rows[:, None, :]).astype(jnp.bfloat...  53.6 us
  transfers between devices with their start and end apart: 2, of which 1 were waited for; matrix products, arithmetic and copies ran while one was open for 0% of the time, Pallas kernels for 0%

profile of v1, /device:TPU:32, one launch (start us, length us, event | category | flops | bytes accessed | tf_op | source)
XLA Modules:
  0.0 860.1 jit_solution(17624780048464373269)
XLA Ops:
  6.5 2.5 broadcast_in_dim.33
  9.1 22.0 %while.21 = (s32[]{:T(128)}, f32[16,64,1024]{2,0,1:T(8,128)}, s32[]{:T(128)}, s32[8]{0:T(128)S(1)}, s32[8]{0:T(128)S(1)}, /*index=5*/bf16[1024,16]{0,1:T(8,128)(...) while((s32[]{:T(128)}, f32[16,64,1024]{2,0,1:T(8,128)}, ...), condition=%wide.region_1.0_spmd, body=%wide.region_0.0_spmd.sunk | while | flops 8454157 | bytes 1052967 | solution.py:24
  12.3 2.1 fusion.18
  17.6 2.1 fusion.18
  23.0 2.1 fusion.18
  28.3 2.1 fusion.18
  31.1 351.6 %all-gather.3.cloned.1.call-done = f32[128,64,1024]{2,0,1:T(8,128)} async-done(((f32[16,64,1024]{2,0,1:T(8,128)}), f32[128,64,1024]{2,0,1:T(8,128)}) %all-gather.3.cloned.1.call-update) | async-done | bytes 33554448 | tf_op jit(solution)/shard_map/all_gather | solution.py:44
  382.7 14.3 %reduce_sum.9 = bf16[16,64,1024]{2,0,1:T(8,128)(2,1)} reduce(f32[8,16,64,1024]{3,1,0,2:T(8,128)} %bitcast.44, f32[]{:T(128)} %constant.51.clone.1), dimensions={0}, to_apply=%region_2.0 | reduce | flops 7340032 | bytes 35651588 | tf_op jit(solution)/shard_map/reduce_sum | solution.py:44
  397.0 1.5 dynamic-slice_convert_fusion
  400.0 1.3 reshape.62
  402.4 7.2 all-to-all-start
  412.5 128.6 %all-reduce.2 = (s32[2048]{0:T(1024)}, s32[2048]{0:T(1024)}) all-reduce(s32[2048]{0:T(1024)S(1)} %dynamic-update-slice, s32[2048]{0:T(1024)S(1)} %dynamic-update-slice.1), channel_id=1, replica_groups=mesh['pair'=32,'lam'=8] {'pair'}, use_global_device_ids=true, to_apply=%add | all-reduce | flops 4096 | bytes 32768
  541.0 1.4 reshape.101
  543.1 1.3 reshape.63
  544.4 308.9 %while.22 = (s32[]{:T(128)}, f32[2,40,20480]{2,1,0:T(8,128)}, s32[8]{0:T(128)S(1)}, bf16[2,2048,40]{1,2,0:T(8,128)(2,1)}, s32[2048]{0:T(1024)}, /*index=5*/bf16[...) while((s32[]{:T(128)}, f32[2,40,20480]{2,1,0:T(8,128)}, ...), condition=%wide.region_4.5_spmd.clone, body=%wide.region_3.4_spmd.clone.sunk | while | flops 853292032 | bytes 59753956 | solution.py:81
  547.7 1.3 gather_fusion
  551.1 6.7 multiply_convert_fusion.2
  557.8 14.8 %reshape.111 = bf16[256,20480,1]{1,0,2:T(8,128)(2,1)} reshape(bf16[256,16,1280]{2,1,0:T(8,128)(2,1)} %multiply_convert_fusion.2) | data formatting | bytes 20971520 | tf_op jit(solution)/shard_map/while/body/eval_jaxpr/convert_element_type | solution.py:70
  572.6 8.8 %convolution_add_fusion.3 = f32[2,40,20480]{2,1,0:T(8,128)} fusion(bf16[256,20480,1]{1,0,2:T(8,128)(2,1)} %reshape.111, f32[2,40,20480]{2,1,0:T(8,128)} %get-tuple-element.347, pred[]{:T(512)S(6)} %compare.3, bf16[2,2048,40]{1,2,0:T(8,128)(2,1)} %get-tuple-element.360, s32[]{:T(128)S(6)} %select_n.68), kind=kOutput, calls=%fused_computation.9.clone.1 | convolution fusion | flops 842137600 | bytes 23633924 | tf_op jit(solution)/shard_map/while/body/eval_jaxpr/qrb,rk->qbk/dot_general | solution.py:76
  584.7 1.3 gather_fusion
  588.1 6.7 multiply_convert_fusion.2
  594.8 14.8 %reshape.111 = bf16[256,20480,1]{1,0,2:T(8,128)(2,1)} reshape(bf16[256,16,1280]{2,1,0:T(8,128)(2,1)} %multiply_convert_fusion.2) | data formatting | bytes 20971520 | tf_op jit(solution)/shard_map/while/body/eval_jaxpr/convert_element_type | solution.py:70
  609.6 10.6 %convolution_add_fusion.3 = f32[2,40,20480]{2,1,0:T(8,128)} fusion(bf16[256,20480,1]{1,0,2:T(8,128)(2,1)} %reshape.111, f32[2,40,20480]{2,1,0:T(8,128)} %get-tuple-element.347, pred[]{:T(512)S(6)} %compare.3, bf16[2,2048,40]{1,2,0:T(8,128)(2,1)} %get-tuple-element.360, s32[]{:T(128)S(6)} %select_n.68), kind=kOutput, calls=%fused_computation.9.clone.1 | convolution fusion | flops 842137600 | bytes 23633924 | tf_op jit(solution)/shard_map/while/body/eval_jaxpr/qrb,rk->qbk/dot_general | solution.py:76
  623.5 1.2 gather_fusion
  624.8 1.2 select_convert_fusion.4
  627.0 6.7 multiply_convert_fusion.2
  633.7 14.8 %reshape.111 = bf16[256,20480,1]{1,0,2:T(8,128)(2,1)} reshape(bf16[256,16,1280]{2,1,0:T(8,128)(2,1)} %multiply_convert_fusion.2) | data formatting | bytes 20971520 | tf_op jit(solution)/shard_map/while/body/eval_jaxpr/convert_element_type | solution.py:70
  648.4 10.6 %convolution_add_fusion.3 = f32[2,40,20480]{2,1,0:T(8,128)} fusion(bf16[256,20480,1]{1,0,2:T(8,128)(2,1)} %reshape.111, f32[2,40,20480]{2,1,0:T(8,128)} %get-tuple-element.347, pred[]{:T(512)S(6)} %compare.3, bf16[2,2048,40]{1,2,0:T(8,128)(2,1)} %get-tuple-element.360, s32[]{:T(128)S(6)} %select_n.68), kind=kOutput, calls=%fused_computation.9.clone.1 | convolution fusion | flops 842137600 | bytes 23633924 | tf_op jit(solution)/shard_map/while/body/eval_jaxpr/qrb,rk->qbk/dot_general | solution.py:76
  662.4 1.3 gather_fusion
  665.8 6.7 multiply_convert_fusion.2
  672.5 14.8 %reshape.111 = bf16[256,20480,1]{1,0,2:T(8,128)(2,1)} reshape(bf16[256,16,1280]{2,1,0:T(8,128)(2,1)} %multiply_convert_fusion.2) | data formatting | bytes 20971520 | tf_op jit(solution)/shard_map/while/body/eval_jaxpr/convert_element_type | solution.py:70
  687.3 10.6 %convolution_add_fusion.3 = f32[2,40,20480]{2,1,0:T(8,128)} fusion(bf16[256,20480,1]{1,0,2:T(8,128)(2,1)} %reshape.111, f32[2,40,20480]{2,1,0:T(8,128)} %get-tuple-element.347, pred[]{:T(512)S(6)} %compare.3, bf16[2,2048,40]{1,2,0:T(8,128)(2,1)} %get-tuple-element.360, s32[]{:T(128)S(6)} %select_n.68), kind=kOutput, calls=%fused_computation.9.clone.1 | convolution fusion | flops 842137600 | bytes 23633924 | tf_op jit(solution)/shard_map/while/body/eval_jaxpr/qrb,rk->qbk/dot_general | solution.py:76
  701.2 1.3 gather_fusion
  704.7 6.7 multiply_convert_fusion.2
  711.4 14.8 %reshape.111 = bf16[256,20480,1]{1,0,2:T(8,128)(2,1)} reshape(bf16[256,16,1280]{2,1,0:T(8,128)(2,1)} %multiply_convert_fusion.2) | data formatting | bytes 20971520 | tf_op jit(solution)/shard_map/while/body/eval_jaxpr/convert_element_type | solution.py:70
  726.1 10.6 %convolution_add_fusion.3 = f32[2,40,20480]{2,1,0:T(8,128)} fusion(bf16[256,20480,1]{1,0,2:T(8,128)(2,1)} %reshape.111, f32[2,40,20480]{2,1,0:T(8,128)} %get-tuple-element.347, pred[]{:T(512)S(6)} %compare.3, bf16[2,2048,40]{1,2,0:T(8,128)(2,1)} %get-tuple-element.360, s32[]{:T(128)S(6)} %select_n.68), kind=kOutput, calls=%fused_computation.9.clone.1 | convolution fusion | flops 842137600 | bytes 23633924 | tf_op jit(solution)/shard_map/while/body/eval_jaxpr/qrb,rk->qbk/dot_general | solution.py:76
  740.0 1.2 gather_fusion
  743.5 6.7 multiply_convert_fusion.2
  750.2 14.8 %reshape.111 = bf16[256,20480,1]{1,0,2:T(8,128)(2,1)} reshape(bf16[256,16,1280]{2,1,0:T(8,128)(2,1)} %multiply_convert_fusion.2) | data formatting | bytes 20971520 | tf_op jit(solution)/shard_map/while/body/eval_jaxpr/convert_element_type | solution.py:70
  765.0 10.6 %convolution_add_fusion.3 = f32[2,40,20480]{2,1,0:T(8,128)} fusion(bf16[256,20480,1]{1,0,2:T(8,128)(2,1)} %reshape.111, f32[2,40,20480]{2,1,0:T(8,128)} %get-tuple-element.347, pred[]{:T(512)S(6)} %compare.3, bf16[2,2048,40]{1,2,0:T(8,128)(2,1)} %get-tuple-element.360, s32[]{:T(128)S(6)} %select_n.68), kind=kOutput, calls=%fused_computation.9.clone.1 | convolution fusion | flops 842137600 | bytes 23633924 | tf_op jit(solution)/shard_map/while/body/eval_jaxpr/qrb,rk->qbk/dot_general | solution.py:76
  778.9 1.2 gather_fusion
  782.3 6.7 multiply_convert_fusion.2
  789.0 14.8 %reshape.111 = bf16[256,20480,1]{1,0,2:T(8,128)(2,1)} reshape(bf16[256,16,1280]{2,1,0:T(8,128)(2,1)} %multiply_convert_fusion.2) | data formatting | bytes 20971520 | tf_op jit(solution)/shard_map/while/body/eval_jaxpr/convert_element_type | solution.py:70
  803.8 10.6 %convolution_add_fusion.3 = f32[2,40,20480]{2,1,0:T(8,128)} fusion(bf16[256,20480,1]{1,0,2:T(8,128)(2,1)} %reshape.111, f32[2,40,20480]{2,1,0:T(8,128)} %get-tuple-element.347, pred[]{:T(512)S(6)} %compare.3, bf16[2,2048,40]{1,2,0:T(8,128)(2,1)} %get-tuple-element.360, s32[]{:T(128)S(6)} %select_n.68), kind=kOutput, calls=%fused_computation.9.clone.1 | convolution fusion | flops 842137600 | bytes 23633924 | tf_op jit(solution)/shard_map/while/body/eval_jaxpr/qrb,rk->qbk/dot_general | solution.py:76
  817.7 1.2 gather_fusion
  821.1 6.7 multiply_convert_fusion.2
  827.8 14.8 %reshape.111 = bf16[256,20480,1]{1,0,2:T(8,128)(2,1)} reshape(bf16[256,16,1280]{2,1,0:T(8,128)(2,1)} %multiply_convert_fusion.2) | data formatting | bytes 20971520 | tf_op jit(solution)/shard_map/while/body/eval_jaxpr/convert_element_type | solution.py:70
  842.6 10.6 %convolution_add_fusion.3 = f32[2,40,20480]{2,1,0:T(8,128)} fusion(bf16[256,20480,1]{1,0,2:T(8,128)(2,1)} %reshape.111, f32[2,40,20480]{2,1,0:T(8,128)} %get-tuple-element.347, pred[]{:T(512)S(6)} %compare.3, bf16[2,2048,40]{1,2,0:T(8,128)(2,1)} %get-tuple-element.360, s32[]{:T(128)S(6)} %select_n.68), kind=kOutput, calls=%fused_computation.9.clone.1 | convolution fusion | flops 842137600 | bytes 23633924 | tf_op jit(solution)/shard_map/while/body/eval_jaxpr/qrb,rk->qbk/dot_general | solution.py:76
  (124 shorter events, 38.1 us)
Async XLA Ops:
  6.5 2.5 copy-start.1
  6.5 2.5 copy-start.2
  6.5 376.1 %all-gather.3.cloned.1.call-start = ((), (), s32[]{:S(2)}) async-start(), calls=%async_computation.1 | async-start | bytes 37748736 | tf_op jit(solution)/shard_map/all_gather | solution.py:44
  382.7 15.9 %copy-start = (bf16[1024,1280]{1,0:T(8,128)(2,1)S(1)}, bf16[1024,1280]{1,0:T(8,128)(2,1)}, u32[]{:S(2)}) copy-start(bf16[1024,1280]{1,0:T(8,128)(2,1)} %param.19) | copy-start | bytes 7864324
  397.0 13.6 %copy-start.5 = (u32[256]{0:T(256)S(1)}, u32[256]{0:T(256)}, u32[]{:S(2)}) copy-start(u32[256]{0:T(256)} %constant.72) | copy-start | bytes 3076
  397.0 15.0 %copy-start.3 = (s32[64]{0:T(128)S(1)}, s32[64]{0:T(128)}, u32[]{:S(2)}) copy-start(s32[64]{0:T(128)} %param.16) | copy-start | bytes 772
  397.0 15.2 %copy-start.4 = (s32[64]{0:T(128)S(1)}, s32[64]{0:T(128)}, u32[]{:S(2)}) copy-start(s32[64]{0:T(128)} %param.17) | copy-start | bytes 772
  402.4 138.6 %all-to-all-start = ((bf16[32,2,2560]{2,1,0:T(2,128)(2,1)}), bf16[32,2,2560]{2,1,0:T(2,128)(2,1)}, u32[]{:S(2)}, u32[]{:S(2)}) async-start(bf16[32,2,2560]{2,1,0:T(2,128)(2,1)} %reshape.100), calls=%async_computation | async-start | bytes 655360 | tf_op jit(solution)/shard_map/all_to_all | solution.py:54
  544.4 3.3 copy-start.6
  572.6 8.8 %copy-start.7 = (s32[8]{0:T(128)S(1)}, s32[8]{0:T(128)}, u32[]{:S(2)}) copy-start(s32[8]{0:T(128)} %copy-done.6) | copy-start | bytes 100 | tf_op jit(solution)/shard_map/while
  581.4 3.3 copy-start.6
  609.6 10.6 %copy-start.7 = (s32[8]{0:T(128)S(1)}, s32[8]{0:T(128)}, u32[]{:S(2)}) copy-start(s32[8]{0:T(128)} %copy-done.6) | copy-start | bytes 100 | tf_op jit(solution)/shard_map/while
  620.2 3.3 copy-start.6
  648.4 10.6 %copy-start.7 = (s32[8]{0:T(128)S(1)}, s32[8]{0:T(128)}, u32[]{:S(2)}) copy-start(s32[8]{0:T(128)} %copy-done.6) | copy-start | bytes 100 | tf_op jit(solution)/shard_map/while
  659.1 3.3 copy-start.6
  687.3 10.6 %copy-start.7 = (s32[8]{0:T(128)S(1)}, s32[8]{0:T(128)}, u32[]{:S(2)}) copy-start(s32[8]{0:T(128)} %copy-done.6) | copy-start | bytes 100 | tf_op jit(solution)/shard_map/while
  697.9 3.3 copy-start.6
  726.1 10.6 %copy-start.7 = (s32[8]{0:T(128)S(1)}, s32[8]{0:T(128)}, u32[]{:S(2)}) copy-start(s32[8]{0:T(128)} %copy-done.6) | copy-start | bytes 100 | tf_op jit(solution)/shard_map/while
  736.8 3.3 copy-start.6
  765.0 10.6 %copy-start.7 = (s32[8]{0:T(128)S(1)}, s32[8]{0:T(128)}, u32[]{:S(2)}) copy-start(s32[8]{0:T(128)} %copy-done.6) | copy-start | bytes 100 | tf_op jit(solution)/shard_map/while
  775.6 3.3 copy-start.6
  803.8 10.6 %copy-start.7 = (s32[8]{0:T(128)S(1)}, s32[8]{0:T(128)}, u32[]{:S(2)}) copy-start(s32[8]{0:T(128)} %copy-done.6) | copy-start | bytes 100 | tf_op jit(solution)/shard_map/while
  814.4 3.3 copy-start.6
  842.6 10.6 %copy-start.7 = (s32[8]{0:T(128)S(1)}, s32[8]{0:T(128)}, u32[]{:S(2)}) copy-start(s32[8]{0:T(128)} %copy-done.6) | copy-start | bytes 100 | tf_op jit(solution)/shard_map/while
Sparse Core Ops, SparseCore 0:
  31.2 351.4 all-gather.2
